TPU v7x, 32 devices: a whole 2x2x4 slice. The times are simulated.
32 devices in a mesh: groups: 2 (over y), seq: 4 (over x, core), fsdp: 4 (over z).
Axes of the slice: x: 2, y: 2, z: 4, core: 2. Of those that a mesh axis runs over, the one named last changes fastest.
Arguments:
- tokens: bfloat16 [16, 512, 1536], P(('groups', 'fsdp'), 'seq'), parts along dimension 0, may hold values from -6 to 6
- in_weight: bfloat16 [1536, 4608], P(None, 'fsdp'), may hold values from -0.15625 to 0.15625
- short_weight: float32 [3, 4608], replicated, may hold values from -3.5 to 3.5
- basis_in: float32 [17, 64], replicated, may hold values from -4 to 4
- basis_bias: float32 [64], replicated, may hold values from -3.140625 to 3.140625
- basis_mid: float32 [64, 64], replicated, may hold values from -1.5 to 1.5
- basis_shift: float32 [64], replicated, may hold values from -3.140625 to 3.140625
- response_out: float32 [2, 64, 1536], P(None, None, 'fsdp'), may hold values from -0.0234375 to 0.0234375
- skip_gain: float32 [1536], P('fsdp'), may hold values from -4 to 4
- block_counts: int32 [16, 4], P(('groups', 'fsdp'), 'seq'), parts along dimension 0, may hold values from 1 to 128, as said below
Outputs:
- mixed: bfloat16 [16, 512, 1536], P(('groups', 'fsdp'), 'seq'), parts along dimension 0
There are 2 independent parts, one for each index of `groups`. A program takes and returns all parts, laid end to end along the dimension named above; an argument that names none is the same for every part. Nothing has to cross between parts.
Inputs may be any that keep to these rules, and one draw needn't show every extreme that they name: `block_counts`: in every table one block holds all 128 tokens and another holds a single token.
All inputs are finite; a program needn't handle non-finite values.
Results may differ from a plain program's by a relative error of at most 0.007.
Values may be sent and summed in bfloat16 or wider, within the bound.
No kernel may reach another device: no remote copies, remote signals or barrier semaphores. Data moves between devices by JAX's collectives and lax.ppermute only.
A program may use at most 128 MiB of HBM per device.

v0:
```python
import jax
import jax.numpy as jnp
from jax import lax
from jax.sharding import PartitionSpec as P


def padded_2(cells, sides, width):
    for axis, dim in sides:
        count = lax.axis_size(axis)
        ends = count - 1
        head = lax.slice_in_dim(cells, 0, width, axis=dim)
        tail = lax.slice_in_dim(cells, cells.shape[dim] - width, cells.shape[dim], axis=dim)
        cells = jnp.concatenate(
            [
                lax.ppermute(tail, axis, [(i, (i + 1) % count) for i in range(ends)]),
                cells,
                lax.ppermute(head, axis, [((i + 1) % count, i) for i in range(ends)]),
            ],
            axis=dim,
        )
    return cells


def filter_basis(lag_values, total_len, basis_in, basis_bias, basis_mid, basis_shift):
    band_count = (basis_in.shape[0] - 1) // 2
    distance = jnp.abs(lag_values)
    periods = (2 ** (jnp.arange(band_count, dtype=jnp.int32) + 2) + 1).astype(jnp.int32)
    angles = (
        2.0
        * jnp.pi
        * (distance[:, None] % periods[None, :]).astype(jnp.float32)
        / periods[None, :].astype(jnp.float32)
    )
    linear = distance.astype(jnp.float32)[:, None] / total_len
    encoded = jnp.concatenate([linear, jnp.cos(angles), jnp.sin(angles)], axis=1)
    hidden = jnp.sin(jnp.dot(encoded, basis_in, precision=lax.Precision.HIGHEST) + basis_bias)
    return jnp.sin(jnp.dot(hidden, basis_mid, precision=lax.Precision.HIGHEST) + basis_shift)


def forward_table(block_len):
    period = 2 * block_len
    frequency = jnp.arange(block_len, dtype=jnp.int32)[:, None]
    samples = jnp.arange(period, dtype=jnp.int32)[None, :]
    phases = 2.0 * jnp.pi / period * (frequency * samples % period).astype(jnp.float32)
    alternate = (1 - 2 * (samples % 2)).astype(jnp.float32)
    real_rows = jnp.cos(phases)
    imag_rows = jnp.where(frequency == 0, alternate, -jnp.sin(phases))
    return jnp.concatenate([real_rows, imag_rows], axis=0)


def inverse_table(block_len):
    period = 2 * block_len
    places = jnp.arange(block_len, dtype=jnp.int32)[:, None]
    frequency = jnp.arange(block_len, dtype=jnp.int32)[None, :]
    phases = 2.0 * jnp.pi / period * (places * frequency % period).astype(jnp.float32)
    alternate = (1 - 2 * (places % 2)).astype(jnp.float32)
    real_cols = jnp.where(frequency == 0, 1.0, 2.0 * jnp.cos(phases)) / period
    imag_cols = jnp.where(frequency == 0, alternate, -2.0 * jnp.sin(phases)) / period
    return jnp.concatenate([real_cols, imag_cols], axis=1)


def packed_product(response, signal, block_len):
    first_slot = (jnp.arange(block_len) == 0)[:, None]
    resp_real = response[..., :block_len, :]
    resp_imag = response[..., block_len:, :]
    sig_real = signal[..., :block_len, :]
    sig_imag = signal[..., block_len:, :]
    cross_term = resp_imag * sig_imag
    prod_real = resp_real * sig_real - jnp.where(first_slot, 0.0, cross_term)
    prod_imag = jnp.where(first_slot, cross_term, resp_real * sig_imag + resp_imag * sig_real)
    return jnp.concatenate([prod_real, prod_imag], axis=-2)


def shards(
    tokens,
    in_weight,
    short_weight,
    basis_in,
    basis_bias,
    basis_mid,
    basis_shift,
    response_out,
    skip_gain,
    block_counts,
):
    seq_dev, block_len, width = tokens.shape
    group_tokens = lax.all_gather(tokens, "fsdp", axis=0, tiled=True)
    group_rows = group_tokens.shape[0]
    local_cols = in_weight.shape[1]
    partial = jnp.dot(
        group_tokens.reshape(group_rows * block_len, width),
        in_weight,
        preferred_element_type=jnp.float32,
    ).astype(jnp.bfloat16)
    partial = partial.reshape(group_rows, block_len, local_cols)
    projected = lax.all_to_all(partial, "fsdp", 0, 2, tiled=True)
    padded = padded_2(projected, (("seq", 1),), 1)
    shorted = (
        short_weight[0] * padded[:, :-2]
        + short_weight[1] * padded[:, 1:-1]
        + short_weight[2] * padded[:, 2:]
    )
    query_gate = shorted[:, :, :width]
    key_part = shorted[:, :, width : 2 * width]
    value_part = shorted[:, :, 2 * width :]
    valid_mask = (jnp.arange(block_len, dtype=jnp.int32)[None, :] < block_counts).astype(
        jnp.float32
    )
    carried = (key_part * value_part * valid_mask[:, :, None]).astype(jnp.bfloat16)
    full_out, full_skip = (
        lax.all_gather(response_out, "fsdp", axis=2, tiled=True),
        lax.all_gather(skip_gain, "fsdp", axis=0, tiled=True),
    )
    stacked_out = full_out.reshape(2 * full_out.shape[1], width)
    seq_count = lax.axis_size("seq")
    position = lax.axis_index("seq")
    total_len = float(seq_count * block_len)
    forward = forward_table(block_len)
    forward_half = forward[:, :block_len]
    inverse = inverse_table(block_len)
    circular = jnp.arange(2 * block_len, dtype=jnp.int32)
    wrapped = jnp.where(circular < block_len, circular, circular - 2 * block_len)

    def kernel_response(offset, out_cols):
        lag_values = offset + wrapped
        basis_rows = filter_basis(
            lag_values, total_len, basis_in, basis_bias, basis_mid, basis_shift
        )
        ahead_mask = (lag_values >= 0).astype(jnp.float32)[:, None]
        paired = jnp.concatenate([basis_rows * ahead_mask, basis_rows * (1.0 - ahead_mask)], axis=1)
        return jnp.dot(
            jnp.dot(forward, paired, precision=lax.Precision.HIGHEST),
            out_cols,
            precision=lax.Precision.HIGHEST,
        )

    def add_block(spectrum, block_rows, start):
        offset = position * block_len - start
        response = kernel_response(offset, stacked_out)
        signal = jnp.einsum(
            "fc,scd->sfd",
            forward_half,
            block_rows.astype(jnp.float32),
            precision=lax.Precision.HIGHEST,
        )
        return spectrum + packed_product(response[None], signal, block_len)

    initial = jnp.zeros((seq_dev, 2 * block_len, width), jnp.float32)
    piece = lax.all_gather(carried, "seq", axis=1, tiled=True)
    piece_rows = piece.shape[1]
    block_total = piece_rows // block_len

    def one_block(block_index, carry):
        block_rows = lax.dynamic_slice_in_dim(piece, block_index * block_len, block_len, 1)
        return add_block(carry, block_rows, block_index * block_len)

    spectrum = lax.fori_loop(0, block_total, one_block, initial)
    conv = jnp.einsum("if,sfd->sid", inverse, spectrum, precision=lax.Precision.HIGHEST)
    return (query_gate * (conv + full_skip * carried.astype(jnp.float32))).astype(jnp.bfloat16)


def solution(mesh):
    placed = (
        P(("groups", "fsdp"), "seq", None),
        P(None, "fsdp"),
        P(),
        P(),
        P(),
        P(),
        P(),
        P(None, None, "fsdp"),
        P("fsdp"),
        P(("groups", "fsdp"), "seq"),
    )
    return jax.shard_map(
        shards,
        mesh=mesh,
        in_specs=placed,
        out_specs=P(("groups", "fsdp"), "seq", None),
        check_vma=False,
    )
```

profile of v0, /device:TPU:2, one launch (start us, length us, event | category | flops | bytes accessed | tf_op | source)
XLA Modules:
  0.0 302.2 jit_solution(2501134679842409714)
XLA Ops:
  7.3 66.4 %all-gather.4.cloned.1.call-done = bf16[8,128,1536]{2,1,0:T(8,128)(2,1)} async-done(((bf16[2,128,1536]{2,1,0:T(8,128)(2,1)}), bf16[8,128,1536]{2,1,0:T(8,128)(2,1)}) %all-gather.4.cloned.1.call-update) | async-done | bytes 3145744 | tf_op jit(solution)/shard_map/all_gather | solution.py:87
  73.7 7.6 %convolution_convert_fusion = bf16[1024,1152]{1,0:T(8,128)(2,1)} fusion(bf16[1024,1536]{1,0:T(8,128)(2,1)} %bitcast.65, bf16[1536,1152]{1,0:T(8,128)(2,1)S(1)} %copy-done), kind=kOutput, calls=%fused_computation.58 | convolution fusion | flops 3625058304 | bytes 9043968 | tf_op jit(solution)/shard_map/dot_general | solution.py:90
  81.3 4.6 %all-to-all-start = ((bf16[8,128,1152]{2,1,0:T(8,128)(2,1)}), bf16[8,128,1152]{2,1,0:T(8,128)(2,1)}, u32[]{:S(2)}, u32[]{:S(2)}) async-start(bf16[8,128,1152]{2,1,0:T(8,128)(2,1)} %bitcast.63), calls=%async_computation | async-start | bytes 4718592 | tf_op jit(solution)/shard_map/all_to_all | solution.py:96
  86.0 54.0 %all-to-all-done = bf16[8,128,1152]{2,1,0:T(8,128)(2,1)} async-done(((bf16[8,128,1152]{2,1,0:T(8,128)(2,1)}), bf16[8,128,1152]{2,1,0:T(8,128)(2,1)}, u32[]{:S(2)}, u32[]{:S(2)}) %all-to-all-start) | async-done | bytes 2359328 | tf_op jit(solution)/shard_map/all_to_all | solution.py:96
  140.0 4.3 %copy.20 = bf16[4,2,128,1152]{2,3,0,1:T(8,128)(2,1)} copy(bf16[4,2,128,1152]{3,2,1,0:T(8,128)(2,1)} %bitcast.2) | data formatting | bytes 4718592 | tf_op jit(solution)/shard_map/all_to_all | solution.py:96
  144.3 5.3 %fusion.56 = (bf16[2,1,4608]{1,2,0:T(8,128)(2,1)}, bf16[2,1,4608]{1,2,0:T(8,128)(2,1)}) fusion(bf16[2,128,4608]{1,2,0:T(8,128)(2,1)} %bitcast.60), kind=kLoop, calls=%fused_computation.111 | loop fusion | bytes 73728 | tf_op jit(solution)/shard_map/slice | solution.py:12
  149.6 2.7 copy.21
  154.2 2.7 copy.23
  156.9 3.6 %collective-permute-start.1 = (bf16[2,1,4608]{2,0,1:T(2,128)(2,1)}, bf16[2,1,4608]{2,0,1:T(2,128)(2,1)}, u32[]{:S(2)}, u32[]{:S(2)}) collective-permute-start(bf16[2,1,4608]{2,0,1:T(2,128)(2,1)} %copy.23), channel_id=1, source_target_pairs={{4,0},{8,4},{12,8},{5,1},{9,5},{13,9},{6,2},{10,6},{14,10},{7,3},{... | collective-permute-start | bytes 55304 | tf_op jit(solution)/shard_map/ppermute | solution.py:17
  162.3 2.6 copy.22
  164.9 2.6 copy.24
  167.6 7.7 %multiply_add_fusion = f32[2,128,4608]{1,2,0:T(8,128)S(1)} fusion(bf16[2,128,4608]{1,2,0:T(8,128)(2,1)} %bitcast.61, bf16[2,1,4608]{1,2,0:T(8,128)(2,1)} %copy.24, bf16[2,1,4608]{1,2,0:T(8,128)(2,1)} %copy.22, f32[4608]{0:T(1024)} %get-tuple-element.353, f32[4608]{0:T(1024)} %get-tuple-element.354, f32[4608]{0:T(1024)} %get-tuple-element.352), kind=kLoop, calls=%fused_computation.57 | loop fusion | flops 16515072 | bytes 7170048 | tf_op jit(solution)/shard_map/add | solution.py:99
  178.5 11.9 %all-gather = f32[4,1,384]{2,1,0:T(1,128)S(1)} all-gather(f32[1,1,384]{2,1,0:T(1,128)S(1)} %reshape.183), channel_id=1, replica_groups=mesh['groups'=2,'seq'=4,'fsdp'=4] {'fsdp'}, dimensions={0}, use_global_device_ids=true | all-gather | bytes 7680 | tf_op jit(solution)/shard_map/all_gather | solution.py:112
  193.3 18.5 %all_gather.13 = f32[2,64,1536]{2,1,0:T(8,128)} all-gather(f32[2,64,384]{2,1,0:T(8,128)} %param.19), channel_id=1, replica_groups=mesh['groups'=2,'seq'=4,'fsdp'=4] {'fsdp'}, dimensions={2}, use_global_device_ids=true | all-gather | bytes 983040 | tf_op jit(solution)/shard_map/all_gather | solution.py:111
  211.8 72.5 %while.16 = (s32[]{:T(128)}, f32[2,256,1536]{2,1,0:T(8,128)}, s32[]{:T(128)}, f32[17,64]{1,0:T(8,128)}, f32[64]{0:T(128)}, /*index=5*/f32[64,64]{1,0:T(8,128)}, ...) while((s32[]{:T(128)}, f32[2,256,1536]{2,1,0:T(8,128)}, ...), condition=%wide.region_1.2_spmd.clone, body=%wide.region_0.1_spmd.clone.sunk | while | flops 1934166400 | bytes 34141608 | solution.py:157
  216.0 2.6 convolution_bitcast_fusion.6
  219.8 2.7 convolution_bitcast_fusion.5
  222.5 2.5 select_subtract_fusion.2
  225.0 4.3 %maximum_add_fusion.2 = f32[2,256,1536]{2,1,0:T(8,128)} fusion(f32[2,128,1536]{2,1,0:T(8,128)} %get-tuple-element.484, f32[2,128,1536]{2,1,0:T(8,128)} %get-tuple-element.485, f32[2,256,1536]{2,1,0:T(8,128)} %get-tuple-element.502, pred[]{:T(512)S(6)} %compare.7), kind=kLoop, calls=%fused_computation.2.clone.1 | loop fusion | flops 2359296 | bytes 9437185 | tf_op jit(solution)/shard_map/while/body/eval_jaxpr/add | solution.py:146
  233.4 2.6 convolution_bitcast_fusion.6
  237.2 2.7 convolution_bitcast_fusion.5
  239.9 2.5 select_subtract_fusion.2
  242.4 5.2 %maximum_add_fusion.2 = f32[2,256,1536]{2,1,0:T(8,128)} fusion(f32[2,128,1536]{2,1,0:T(8,128)} %get-tuple-element.484, f32[2,128,1536]{2,1,0:T(8,128)} %get-tuple-element.485, f32[2,256,1536]{2,1,0:T(8,128)} %get-tuple-element.502, pred[]{:T(512)S(6)} %compare.7), kind=kLoop, calls=%fused_computation.2.clone.1 | loop fusion | flops 2359296 | bytes 9437185 | tf_op jit(solution)/shard_map/while/body/eval_jaxpr/add | solution.py:146
  251.7 2.6 convolution_bitcast_fusion.6
  255.6 2.7 convolution_bitcast_fusion.5
  258.3 2.5 select_subtract_fusion.2
  260.7 5.2 %maximum_add_fusion.2 = f32[2,256,1536]{2,1,0:T(8,128)} fusion(f32[2,128,1536]{2,1,0:T(8,128)} %get-tuple-element.484, f32[2,128,1536]{2,1,0:T(8,128)} %get-tuple-element.485, f32[2,256,1536]{2,1,0:T(8,128)} %get-tuple-element.502, pred[]{:T(512)S(6)} %compare.7), kind=kLoop, calls=%fused_computation.2.clone.1 | loop fusion | flops 2359296 | bytes 9437185 | tf_op jit(solution)/shard_map/while/body/eval_jaxpr/add | solution.py:146
  270.1 2.6 convolution_bitcast_fusion.6
  273.9 2.7 convolution_bitcast_fusion.5
  276.6 2.5 select_subtract_fusion.2
  279.1 5.2 %maximum_add_fusion.2 = f32[2,256,1536]{2,1,0:T(8,128)} fusion(f32[2,128,1536]{2,1,0:T(8,128)} %get-tuple-element.484, f32[2,128,1536]{2,1,0:T(8,128)} %get-tuple-element.485, f32[2,256,1536]{2,1,0:T(8,128)} %get-tuple-element.502, pred[]{:T(512)S(6)} %compare.7), kind=kLoop, calls=%fused_computation.2.clone.1 | loop fusion | flops 2359296 | bytes 9437185 | tf_op jit(solution)/shard_map/while/body/eval_jaxpr/add | solution.py:146
  284.3 8.8 %fusion.32 = bf16[2,128,1536]{1,2,0:T(8,128)(2,1)} fusion(f32[2,128,4608]{1,2,0:T(8,128)} %copy-done.3, f32[2,256,1536]{2,1,0:T(8,128)} %get-tuple-element.280, bf16[2,128,1536]{1,2,0:T(8,128)(2,1)} %fusion.31, f32[1536]{0:T(1024)S(1)} %reshape.184, f32[128,128]{1,0:T(8,128)} %get-tuple-element.392, f32[128,128]{1,0:T(8,128)} %get-tuple-element.391), kind=kOutput, calls=%fused_computation.67 | convolution fusion | flops 1209958400 | bytes 6428672 | tf_op jit(solution)/shard_map/if,sfd->sid/dot_general | solution.py:158
  (91 shorter events, 34.3 us)
Async XLA Ops:
  6.5 67.2 %copy-start = (bf16[1536,1152]{1,0:T(8,128)(2,1)S(1)}, bf16[1536,1152]{1,0:T(8,128)(2,1)}, u32[]{:S(2)}) copy-start(bf16[1536,1152]{1,0:T(8,128)(2,1)} %param.13) | copy-start | bytes 10616836
  6.5 67.2 %all-gather.4.cloned.1.call-start = ((), (), s32[]{:S(2)}) async-start(), calls=%async_computation.1 | async-start | bytes 3932160 | tf_op jit(solution)/shard_map/all_gather | solution.py:87
  81.3 4.7 %copy-start.5 = (s32[2,1]{0,1:T(1,128)S(1)}, s32[2,1]{0,1:T(1,128)}, u32[]{:S(2)}) copy-start(s32[2,1]{0,1:T(1,128)} %param.21) | copy-start | bytes 28
  81.3 58.8 %all-to-all-start = ((bf16[8,128,1152]{2,1,0:T(8,128)(2,1)}), bf16[8,128,1152]{2,1,0:T(8,128)(2,1)}, u32[]{:S(2)}, u32[]{:S(2)}) async-start(bf16[8,128,1152]{2,1,0:T(8,128)(2,1)} %bitcast.63), calls=%async_computation | async-start | bytes 4718592 | tf_op jit(solution)/shard_map/all_to_all | solution.py:96
  85.9 125.9 %all-gather.6.cloned.1.call-start = ((), (), s32[]{:S(2)}) async-start(), calls=%async_computation.2 | async-start | bytes 3932160 | tf_op jit(solution)/shard_map/all_gather | solution.py:149
  152.3 10.0 %collective-permute-start = (bf16[2,1,4608]{2,0,1:T(2,128)(2,1)}, bf16[2,1,4608]{2,0,1:T(2,128)(2,1)}, u32[]{:S(2)}, u32[]{:S(2)}) collective-permute-start(bf16[2,1,4608]{2,0,1:T(2,128)(2,1)} %copy.21), channel_id=1, source_target_pairs={{0,4},{4,8},{8,12},{1,5},{5,9},{9,13},{2,6},{6,10},{10,14},{3,7},{... | collective-permute-start | bytes 55304 | tf_op jit(solution)/shard_map/ppermute | solution.py:15
  156.9 8.0 %collective-permute-start.1 = (bf16[2,1,4608]{2,0,1:T(2,128)(2,1)}, bf16[2,1,4608]{2,0,1:T(2,128)(2,1)}, u32[]{:S(2)}, u32[]{:S(2)}) collective-permute-start(bf16[2,1,4608]{2,0,1:T(2,128)(2,1)} %copy.23), channel_id=1, source_target_pairs={{4,0},{8,4},{12,8},{5,1},{9,5},{13,9},{6,2},{10,6},{14,10},{7,3},{... | collective-permute-start | bytes 55304 | tf_op jit(solution)/shard_map/ppermute | solution.py:17
  175.2 2.1 copy-start.3
  177.4 1.1 copy-start.4
  219.8 2.7 copy-start.1
  219.8 2.7 copy-start.2
  237.2 2.7 copy-start.1
  237.2 2.7 copy-start.2
  255.6 2.7 copy-start.1
  255.6 2.7 copy-start.2
  273.9 2.7 copy-start.1
  273.9 2.7 copy-start.2
Sparse Core Ops, SparseCore 0:
  8.9 64.7 all-gather.3
  178.6 26.8 all-gather.5
where the time goes:
time: 304 us; the launch traced here: 302 us
  waiting for transfers between devices  121 us (40%)
  matrix products  52.3 us (17%)
  other arithmetic  42.7 us (14%)
  local copies, waits for them, and re-layouts  31.5 us (10%)
  blocking collectives  30.4 us (10%)
  between operations  13.5 us (4%)
  starting transfers between devices  10.2 us (3%)
    all_gather x1, waiting for transfers between devices, shards(): group_tokens = lax.all_gather(tokens, 'fsdp', axis=0, tiled=True)  66.4 us
    all_to_all x1, waiting for transfers between devices, shards(): projected = lax.all_to_all(partial, 'fsdp', 0, 2, tiled=True)  54 us
    add x4, other arithmetic, add_block(): return spectrum + packed_product(response[None], signal, block_len)  19.9 us
    all_gather x1, blocking collectives, shards(): lax.all_gather(response_out, 'fsdp', axis=2, tiled=True)  18.5 us
    all_gather x1, blocking collectives, shards(): lax.all_gather(skip_gain, 'fsdp', axis=0, tiled=True)  11.9 us
    dot_general x4, matrix products, add_block(): jnp.einsum('fc,scd->sfd', forward_half, block_rows.astype(jnp.float32), p...  10.7 us
    dot_general x4, matrix products, kernel_response(): jnp.dot(jnp.dot(forward, paired, precision=lax.Precision.HIGHEST), out_co...  10.3 us
    sub x4, other arithmetic, packed_product(): prod_real = resp_real * sig_real - jnp.where(first_slot, 0.0, cross_term)  9.89 us
  transfers between devices with their start and end apart: 5, of which 2 were waited for; matrix products, arithmetic and copies ran while one was open for 3% of the time, Pallas kernels for 0%

commit v1 on v0

--- a/solution.py
+++ b/solution.py
@@ -84,7 +84,12 @@
     block_counts,
 ):
     seq_dev, block_len, width = tokens.shape
-    group_tokens = lax.all_gather(tokens, "fsdp", axis=0, tiled=True)
+    ring = [tokens]
+    for hop in range(3):
+        ring.append(lax.ppermute(ring[-1], "fsdp", [(dev, (dev + 1) % 4) for dev in range(4)]))
+    group_tokens = jnp.roll(
+        jnp.concatenate(ring[::-1], axis=0), (lax.axis_index("fsdp") + 1) * ring[0].shape[0], axis=0
+    )
     group_rows = group_tokens.shape[0]
     local_cols = in_weight.shape[1]
     partial = jnp.dot(

time: 304 us -> 300 us (0.987)
  waiting for transfers between devices: 121 us -> 111 us
  local copies, waits for them, and re-layouts: 31.5 us -> 37.7 us
    all_gather x1 -> x0, waiting for transfers between devices: 66.4 us -> none  [shards(): group_tokens = lax.all_gather(tokens, 'fsdp', axis=0, tiled=True)]
    ppermute x0 -> x3, waiting for transfers between devices: none -> 59.8 us  [shards(): lax.ppermute(ring[-1], 'fsdp', [(dev, (dev + 1) % 4) for dev in range(4)])]
    unnamed x10 -> x23, local copies, waits for them, and re-layouts: 2.14 us -> 7.95 us
  transfers between devices with their start and end apart: 5 -> 7, of which waited for: 2 -> 4; matrix products, arithmetic and copies ran while one was open for 3% -> 3% of each run, Pallas kernels for 0% -> 0%
where the time goes in v1:
time: 300 us; the launch traced here: 298 us
  waiting for transfers between devices  111 us (37%)
  matrix products  50.2 us (17%)
  other arithmetic  42.8 us (14%)
  local copies, waits for them, and re-layouts  37.7 us (13%)
  blocking collectives  30.4 us (10%)
  between operations  13.6 us (5%)
  starting transfers between devices  11.8 us (4%)
    ppermute x3, waiting for transfers between devices, shards(): lax.ppermute(ring[-1], 'fsdp', [(dev, (dev + 1) % 4) for dev in range(4)])  59.8 us
    all_to_all x1, waiting for transfers between devices, shards(): projected = lax.all_to_all(partial, 'fsdp', 0, 2, tiled=True)  51.4 us
    add x4, other arithmetic, add_block(): return spectrum + packed_product(response[None], signal, block_len)  20 us
    all_gather x1, blocking collectives, shards(): lax.all_gather(response_out, 'fsdp', axis=2, tiled=True)  18.5 us
    all_gather x1, blocking collectives, shards(): lax.all_gather(skip_gain, 'fsdp', axis=0, tiled=True)  11.9 us
    dot_general x4, matrix products, add_block(): jnp.einsum('fc,scd->sfd', forward_half, block_rows.astype(jnp.float32), p...  10.7 us
    dot_general x4, matrix products, kernel_response(): jnp.dot(jnp.dot(forward, paired, precision=lax.Precision.HIGHEST), out_co...  10.3 us
    sub x4, other arithmetic, packed_product(): prod_real = resp_real * sig_real - jnp.where(first_slot, 0.0, cross_term)  9.95 us
  transfers between devices with their start and end apart: 7, of which 4 were waited for; matrix products, arithmetic and copies ran while one was open for 3% of the time, Pallas kernels for 0%

profile of v1, /device:TPU:2, one launch (start us, length us, event | category | flops | bytes accessed | tf_op | source)
XLA Modules:
  0.0 298.0 jit_solution(15228415627406417067)
XLA Ops:
  8.1 19.8 %collective-permute-done = bf16[2,128,1536]{2,1,0:T(8,128)(2,1)S(1)} collective-permute-done((bf16[2,128,1536]{2,1,0:T(8,128)(2,1)}, bf16[2,128,1536]{2,1,0:T(8,128)(2,1)S(1)}, u32[]{:S(2)}, u32[]{:S(2)}) %collective-permute-start) | collective-permute-done | bytes 786464 | tf_op jit(solution)/shard_map/ppermute | solution.py:89
  28.8 20.4 %collective-permute-done.1 = bf16[2,128,1536]{2,1,0:T(8,128)(2,1)} collective-permute-done((bf16[2,128,1536]{2,1,0:T(8,128)(2,1)S(1)}, bf16[2,128,1536]{2,1,0:T(8,128)(2,1)}, u32[]{:S(2)}, u32[]{:S(2)}) %collective-permute-start.1) | collective-permute-done | bytes 786464 | tf_op jit(solution)/shard_map/ppermute | solution.py:89
  49.2 19.7 %collective-permute-done.2 = bf16[2,128,1536]{2,1,0:T(8,128)(2,1)} collective-permute-done((bf16[2,128,1536]{2,1,0:T(8,128)(2,1)}, bf16[2,128,1536]{2,1,0:T(8,128)(2,1)}, u32[]{:S(2)}, u32[]{:S(2)}) %collective-permute-start.2) | collective-permute-done | bytes 786464 | tf_op jit(solution)/shard_map/ppermute | solution.py:89
  74.1 5.4 %convolution_convert_fusion = bf16[1024,1152]{1,0:T(8,128)(2,1)} fusion(bf16[1024,1536]{1,0:T(8,128)(2,1)S(1)} %bitcast.63, bf16[1536,1152]{1,0:T(8,128)(2,1)S(1)} %copy-done), kind=kOutput, calls=%fused_computation.58 | convolution fusion | flops 3625058304 | bytes 9043968 | tf_op jit(solution)/shard_map/dot_general | solution.py:95
  79.5 4.6 %all-to-all-start = ((bf16[8,128,1152]{2,1,0:T(8,128)(2,1)}), bf16[8,128,1152]{2,1,0:T(8,128)(2,1)}, u32[]{:S(2)}, u32[]{:S(2)}) async-start(bf16[8,128,1152]{2,1,0:T(8,128)(2,1)} %bitcast.64), calls=%async_computation | async-start | bytes 4718592 | tf_op jit(solution)/shard_map/all_to_all | solution.py:101
  84.3 51.4 %all-to-all-done = bf16[8,128,1152]{2,1,0:T(8,128)(2,1)} async-done(((bf16[8,128,1152]{2,1,0:T(8,128)(2,1)}), bf16[8,128,1152]{2,1,0:T(8,128)(2,1)}, u32[]{:S(2)}, u32[]{:S(2)}) %all-to-all-start) | async-done | bytes 2359328 | tf_op jit(solution)/shard_map/all_to_all | solution.py:101
  135.7 4.3 %copy.20 = bf16[4,2,128,1152]{2,3,0,1:T(8,128)(2,1)} copy(bf16[4,2,128,1152]{3,2,1,0:T(8,128)(2,1)} %bitcast.2) | data formatting | bytes 4718592 | tf_op jit(solution)/shard_map/all_to_all | solution.py:101
  140.0 5.2 %fusion.56 = (bf16[2,1,4608]{1,2,0:T(8,128)(2,1)}, bf16[2,1,4608]{1,2,0:T(8,128)(2,1)}) fusion(bf16[2,128,4608]{1,2,0:T(8,128)(2,1)} %bitcast.60), kind=kLoop, calls=%fused_computation.120 | loop fusion | bytes 73728 | tf_op jit(solution)/shard_map/slice | solution.py:12
  145.3 2.7 copy.21
  149.9 2.7 copy.23
  152.6 3.6 %collective-permute-start.4 = (bf16[2,1,4608]{2,0,1:T(2,128)(2,1)}, bf16[2,1,4608]{2,0,1:T(2,128)(2,1)}, u32[]{:S(2)}, u32[]{:S(2)}) collective-permute-start(bf16[2,1,4608]{2,0,1:T(2,128)(2,1)} %copy.23), channel_id=1, source_target_pairs={{4,0},{8,4},{12,8},{5,1},{9,5},{13,9},{6,2},{10,6},{14,10},{7,3},{... | collective-permute-start | bytes 55304 | tf_op jit(solution)/shard_map/ppermute | solution.py:17
  158.0 2.6 copy.22
  160.6 2.7 copy.24
  163.3 7.6 %multiply_add_fusion = f32[2,128,4608]{1,2,0:T(8,128)S(1)} fusion(bf16[2,128,4608]{1,2,0:T(8,128)(2,1)} %bitcast.61, bf16[2,1,4608]{1,2,0:T(8,128)(2,1)} %copy.24, bf16[2,1,4608]{1,2,0:T(8,128)(2,1)} %copy.22, f32[4608]{0:T(1024)} %get-tuple-element.353, f32[4608]{0:T(1024)} %get-tuple-element.354, f32[4608]{0:T(1024)} %get-tuple-element.352), kind=kLoop, calls=%fused_computation.57 | loop fusion | flops 16515072 | bytes 7170048 | tf_op jit(solution)/shard_map/add | solution.py:104
  174.2 11.9 %all-gather = f32[4,1,384]{2,1,0:T(1,128)S(1)} all-gather(f32[1,1,384]{2,1,0:T(1,128)S(1)} %reshape.183), channel_id=1, replica_groups=mesh['groups'=2,'seq'=4,'fsdp'=4] {'fsdp'}, dimensions={0}, use_global_device_ids=true | all-gather | bytes 7680 | tf_op jit(solution)/shard_map/all_gather | solution.py:117
  189.0 18.5 %all_gather.9 = f32[2,64,1536]{2,1,0:T(8,128)} all-gather(f32[2,64,384]{2,1,0:T(8,128)} %param.19), channel_id=1, replica_groups=mesh['groups'=2,'seq'=4,'fsdp'=4] {'fsdp'}, dimensions={2}, use_global_device_ids=true | all-gather | bytes 983040 | tf_op jit(solution)/shard_map/all_gather | solution.py:116
  207.5 72.6 %while.16 = (s32[]{:T(128)}, f32[2,256,1536]{2,1,0:T(8,128)}, s32[]{:T(128)}, f32[17,64]{1,0:T(8,128)}, f32[64]{0:T(128)}, /*index=5*/f32[64,64]{1,0:T(8,128)}, ...) while((s32[]{:T(128)}, f32[2,256,1536]{2,1,0:T(8,128)}, ...), condition=%wide.region_1.2_spmd.clone, body=%wide.region_0.1_spmd.clone.sunk | while | flops 1934166400 | bytes 34141608 | solution.py:162
  211.6 2.6 convolution_bitcast_fusion.6
  215.5 2.7 convolution_bitcast_fusion.5
  220.7 4.3 %maximum_add_fusion.2 = f32[2,256,1536]{2,1,0:T(8,128)} fusion(f32[2,128,1536]{2,1,0:T(8,128)} %get-tuple-element.484, f32[2,128,1536]{2,1,0:T(8,128)} %get-tuple-element.485, f32[2,256,1536]{2,1,0:T(8,128)} %get-tuple-element.502, pred[]{:T(512)S(6)} %compare.8), kind=kLoop, calls=%fused_computation.2.clone.1 | loop fusion | flops 2359296 | bytes 9437185 | tf_op jit(solution)/shard_map/while/body/eval_jaxpr/add | solution.py:151
  229.0 2.6 convolution_bitcast_fusion.6
  232.9 2.7 convolution_bitcast_fusion.5
  235.6 2.5 select_subtract_fusion.2
  238.1 5.2 %maximum_add_fusion.2 = f32[2,256,1536]{2,1,0:T(8,128)} fusion(f32[2,128,1536]{2,1,0:T(8,128)} %get-tuple-element.484, f32[2,128,1536]{2,1,0:T(8,128)} %get-tuple-element.485, f32[2,256,1536]{2,1,0:T(8,128)} %get-tuple-element.502, pred[]{:T(512)S(6)} %compare.8), kind=kLoop, calls=%fused_computation.2.clone.1 | loop fusion | flops 2359296 | bytes 9437185 | tf_op jit(solution)/shard_map/while/body/eval_jaxpr/add | solution.py:151
  247.4 2.6 convolution_bitcast_fusion.6
  251.3 2.7 convolution_bitcast_fusion.5
  254.0 2.5 select_subtract_fusion.2
  256.5 5.2 %maximum_add_fusion.2 = f32[2,256,1536]{2,1,0:T(8,128)} fusion(f32[2,128,1536]{2,1,0:T(8,128)} %get-tuple-element.484, f32[2,128,1536]{2,1,0:T(8,128)} %get-tuple-element.485, f32[2,256,1536]{2,1,0:T(8,128)} %get-tuple-element.502, pred[]{:T(512)S(6)} %compare.8), kind=kLoop, calls=%fused_computation.2.clone.1 | loop fusion | flops 2359296 | bytes 9437185 | tf_op jit(solution)/shard_map/while/body/eval_jaxpr/add | solution.py:151
  265.8 2.6 convolution_bitcast_fusion.6
  269.7 2.7 convolution_bitcast_fusion.5
  274.9 5.2 %maximum_add_fusion.2 = f32[2,256,1536]{2,1,0:T(8,128)} fusion(f32[2,128,1536]{2,1,0:T(8,128)} %get-tuple-element.484, f32[2,128,1536]{2,1,0:T(8,128)} %get-tuple-element.485, f32[2,256,1536]{2,1,0:T(8,128)} %get-tuple-element.502, pred[]{:T(512)S(6)} %compare.8), kind=kLoop, calls=%fused_computation.2.clone.1 | loop fusion | flops 2359296 | bytes 9437185 | tf_op jit(solution)/shard_map/while/body/eval_jaxpr/add | solution.py:151
  280.1 8.8 %fusion.32 = bf16[2,128,1536]{1,2,0:T(8,128)(2,1)} fusion(f32[2,128,4608]{1,2,0:T(8,128)} %copy-done.3, f32[2,256,1536]{2,1,0:T(8,128)} %get-tuple-element.280, bf16[2,128,1536]{1,2,0:T(8,128)(2,1)} %fusion.31, f32[1536]{0:T(1024)S(1)} %reshape.184, f32[128,128]{1,0:T(8,128)} %get-tuple-element.392, f32[128,128]{1,0:T(8,128)} %get-tuple-element.391), kind=kOutput, calls=%fused_computation.67 | convolution fusion | flops 1209958400 | bytes 6428672 | tf_op jit(solution)/shard_map/if,sfd->sid/dot_general | solution.py:163
  (109 shorter events, 46.2 us)
Async XLA Ops:
  6.5 67.6 %copy-start = (bf16[1536,1152]{1,0:T(8,128)(2,1)S(1)}, bf16[1536,1152]{1,0:T(8,128)(2,1)}, u32[]{:S(2)}) copy-start(bf16[1536,1152]{1,0:T(8,128)(2,1)} %param.13) | copy-start | bytes 10616836
  6.5 21.4 %collective-permute-start = (bf16[2,128,1536]{2,1,0:T(8,128)(2,1)}, bf16[2,128,1536]{2,1,0:T(8,128)(2,1)S(1)}, u32[]{:S(2)}, u32[]{:S(2)}) collective-permute-start(bf16[2,128,1536]{2,1,0:T(8,128)(2,1)} %param.12), channel_id=1, source_target_pairs={{0,1},{1,2},{2,3},{3,0},{4,5},{5,6},{6,7},{7,4},{8,9},{9,10},{10,1... | collective-permute-start | bytes 2359304 | tf_op jit(solution)/shard_map/ppermute | solution.py:89
  27.9 0.9 copy-start.5
  28.8 20.4 %collective-permute-start.1 = (bf16[2,128,1536]{2,1,0:T(8,128)(2,1)S(1)}, bf16[2,128,1536]{2,1,0:T(8,128)(2,1)}, u32[]{:S(2)}, u32[]{:S(2)}) collective-permute-start(bf16[2,128,1536]{2,1,0:T(8,128)(2,1)S(1)} %collective-permute-done), channel_id=1, source_target_pairs={{0,1},{1,2},{2,3},{3,0},{4,5},{5,6},{6,7},{7,4},{8,9},{9,10},{10,1... | collective-permute-start | bytes 2359304 | tf_op jit(solution)/shard_map/ppermute | solution.py:89
  49.2 19.7 %collective-permute-start.2 = (bf16[2,128,1536]{2,1,0:T(8,128)(2,1)}, bf16[2,128,1536]{2,1,0:T(8,128)(2,1)}, u32[]{:S(2)}, u32[]{:S(2)}) collective-permute-start(bf16[2,128,1536]{2,1,0:T(8,128)(2,1)} %collective-permute-done.1), channel_id=1, source_target_pairs={{0,1},{1,2},{2,3},{3,0},{4,5},{5,6},{6,7},{7,4},{8,9},{9,10},{10,1... | collective-permute-start | bytes 2359304 | tf_op jit(solution)/shard_map/ppermute | solution.py:89
  49.2 22.0 %copy-start.6 = (bf16[2,128,1536]{2,1,0:T(8,128)(2,1)S(1)}, bf16[2,128,1536]{2,1,0:T(8,128)(2,1)}, u32[]{:S(2)}) copy-start(bf16[2,128,1536]{2,1,0:T(8,128)(2,1)} %copy-done.5) | copy-start | bytes 2359300
  49.2 22.1 %copy-start.4 = (bf16[2,128,1536]{2,1,0:T(8,128)(2,1)S(1)}, bf16[2,128,1536]{2,1,0:T(8,128)(2,1)}, u32[]{:S(2)}) copy-start(bf16[2,128,1536]{2,1,0:T(8,128)(2,1)} %param.12) | copy-start | bytes 2359300
  79.5 4.7 %copy-start.8 = (s32[2,1]{0,1:T(1,128)S(1)}, s32[2,1]{0,1:T(1,128)}, u32[]{:S(2)}) copy-start(s32[2,1]{0,1:T(1,128)} %param.21) | copy-start | bytes 28
  79.5 56.2 %all-to-all-start = ((bf16[8,128,1152]{2,1,0:T(8,128)(2,1)}), bf16[8,128,1152]{2,1,0:T(8,128)(2,1)}, u32[]{:S(2)}, u32[]{:S(2)}) async-start(bf16[8,128,1152]{2,1,0:T(8,128)(2,1)} %bitcast.64), calls=%async_computation | async-start | bytes 4718592 | tf_op jit(solution)/shard_map/all_to_all | solution.py:101
  84.2 123.3 %all-gather.3.cloned.1.call-start = ((), (), s32[]{:S(2)}) async-start(), calls=%async_computation.1 | async-start | bytes 3932160 | tf_op jit(solution)/shard_map/all_gather | solution.py:154
  148.0 10.0 %collective-permute-start.3 = (bf16[2,1,4608]{2,0,1:T(2,128)(2,1)}, bf16[2,1,4608]{2,0,1:T(2,128)(2,1)}, u32[]{:S(2)}, u32[]{:S(2)}) collective-permute-start(bf16[2,1,4608]{2,0,1:T(2,128)(2,1)} %copy.21), channel_id=1, source_target_pairs={{0,4},{4,8},{8,12},{1,5},{5,9},{9,13},{2,6},{6,10},{10,14},{3,7},{... | collective-permute-start | bytes 55304 | tf_op jit(solution)/shard_map/ppermute | solution.py:15
  152.6 8.1 %collective-permute-start.4 = (bf16[2,1,4608]{2,0,1:T(2,128)(2,1)}, bf16[2,1,4608]{2,0,1:T(2,128)(2,1)}, u32[]{:S(2)}, u32[]{:S(2)}) collective-permute-start(bf16[2,1,4608]{2,0,1:T(2,128)(2,1)} %copy.23), channel_id=1, source_target_pairs={{4,0},{8,4},{12,8},{5,1},{9,5},{13,9},{6,2},{10,6},{14,10},{7,3},{... | collective-permute-start | bytes 55304 | tf_op jit(solution)/shard_map/ppermute | solution.py:17
  170.9 2.1 copy-start.3
  173.0 1.1 copy-start.7
  215.5 2.7 copy-start.1
  215.5 2.7 copy-start.2
  232.9 2.7 copy-start.1
  232.9 2.7 copy-start.2
  251.3 2.7 copy-start.1
  251.3 2.7 copy-start.2
  269.7 2.7 copy-start.1
  269.7 2.7 copy-start.2
Sparse Core Ops, SparseCore 0:
  174.2 26.8 all-gather.2
